TPU v7x, 32 devices: a whole 2x2x4 slice. The times are simulated.
32 devices in a mesh: groups: 2 (over x), state: 16 (over z, y, core).
Axes of the slice: x: 2, y: 2, z: 4, core: 2. Of those that a mesh axis runs over, the one named last changes fastest.
Arguments:
- forward_probs: float32 [256, 8, 8192], P('groups', None, 'state'), parts along dimension 0, may hold values from 0.1 to 10
- token_ids: int32 [256, 8], P('groups'), parts along dimension 0, may hold values from 0 to 16383
- transition: bfloat16 [8192, 8192], P('state'), may hold values from 0.1 to 10
- emission: bfloat16 [8192, 16384], P('state'), may hold values from 0.05 to 20
Outputs:
- backward_probs: float32 [256, 8, 8192], P('groups', None, 'state'), parts along dimension 0
- trans_counts: float32 [16384, 8192], P(('groups', 'state')), parts along dimension 0
There are 2 independent parts, one for each index of `groups`. A program takes and returns all parts, laid end to end along the dimension named above; an argument that names none is the same for every part. Nothing has to cross between parts.
All inputs are finite; a program needn't handle non-finite values.
Results may differ from a plain program's by a relative error of at most 0.00031.
Values may be sent and summed in bfloat16 or wider, within the bound.
No kernel may reach another device: no remote copies, remote signals or barrier semaphores. Data moves between devices by JAX's collectives and lax.ppermute only.
A program may use at most 192 MiB of HBM per device.

v0:
```python
import jax
import jax.numpy as jnp
from jax import lax
from jax.sharding import PartitionSpec as P


def on_device(forward_probs, token_ids, transition, emission):
    state_rows = transition.shape[0]
    states = transition.shape[1]
    seq_count = token_ids.shape[0]
    step_count = token_ids.shape[1]
    emitted = jnp.take(emission, token_ids.reshape(-1), axis=1).astype(jnp.float32)
    emitted = emitted.reshape(state_rows, seq_count, step_count)
    backward = jnp.ones((seq_count, state_rows), jnp.float32)
    weighted = (emitted[:, :, step_count - 1].T * backward).astype(jnp.bfloat16)
    backs = [backward]
    stored = []
    scales = []
    for t in range(step_count - 2, -1, -1):
        whole = lax.all_gather(weighted, "state", axis=1, tiled=True)
        scale_sum = lax.psum(jnp.sum(weighted.astype(jnp.float32), axis=1), "state")
        product = lax.dot_general(
            whole, transition, (((1,), (1,)), ((), ())), preferred_element_type=jnp.float32
        )
        backward = product / scale_sum[:, None]
        stored.append(whole)
        scales.append(scale_sum)
        backs.append(backward)
        if t > 0:
            weighted = (emitted[:, :, t].T * backward).astype(jnp.bfloat16)
    backs = backs[::-1]
    stored = stored[::-1]
    scales = scales[::-1]
    backward_probs = jnp.stack(backs, axis=1)
    partial_norms = jnp.sum(
        forward_probs[:, : step_count - 1, :] * backward_probs[:, : step_count - 1, :], axis=2
    )
    norm_sums = lax.psum(partial_norms, "state")
    shares = []
    for t in range(step_count - 1):
        shares.append(
            (forward_probs[:, t, :] / (scales[t] * norm_sums[:, t])[:, None]).astype(jnp.bfloat16)
        )
    share_mat = jnp.concatenate(shares, axis=0)
    vector_mat = jnp.concatenate(stored, axis=0)
    moments = lax.dot_general(
        share_mat, vector_mat, (((0,), (0,)), ((), ())), preferred_element_type=jnp.float32
    )
    factor = float(states) * float(states) / float(seq_count * (step_count - 1))
    trans_counts = transition.astype(jnp.float32) * moments * factor
    return (backward_probs, trans_counts)


def solution(mesh):
    placed = (P("groups", None, "state"), P("groups", None), P("state", None), P("state", None))
    return jax.shard_map(
        on_device,
        mesh=mesh,
        in_specs=placed,
        out_specs=(P("groups", None, "state"), P(("groups", "state"), None)),
        check_vma=False,
    )
```

profile of v0, /device:TPU:0, one launch (start us, length us, event | category | flops | bytes accessed | tf_op | source)
XLA Modules:
  0.0 467.3 jit_solution(17282354931980316428)
XLA Ops:
  7.9 0.8 copy.15
  8.8 22.4 %copy.16 = bf16[512,16384]{0,1:T(8,128)(2,1)} copy(bf16[512,16384]{1,0:T(8,128)(2,1)} %param.7) | data formatting | bytes 33554432 | tf_op args[3]
  31.2 11.9 %gather_fusion = bf16[1024,512]{1,0:T(8,128)(2,1)S(1)} fusion(bf16[512,16384]{0,1:T(8,128)(2,1)} %copy.16, s32[1024]{0:T(1024)S(1)} %broadcast_clamp_fusion), kind=kCustom, calls=%fused_computation | custom fusion | bytes 2101248 | tf_op jit(solution)/shard_map/jit(_take)/gather | solution.py:12
  43.2 0.8 fusion.41
  44.0 0.9 copy-done.9
  45.7 1.0 convert_reduce_fusion.6
  46.7 35.4 %psum.56 = f32[128]{0:T(128)S(1)} all-reduce(f32[128]{0:T(128)S(1)} %convert_reduce_fusion.6), channel_id=1, replica_groups=mesh['groups'=2,'state'=16] {'state'}, use_global_device_ids=true, to_apply=%region_1.2 | all-reduce | flops 128 | bytes 1024 | tf_op jit(solution)/shard_map/psum | solution.py:21
  82.1 7.6 %all-gather.8.cloned.1.call-done = bf16[128,8192]{1,0:T(8,128)(2,1)} async-done(((bf16[128,512]{1,0:T(8,128)(2,1)}), bf16[128,8192]{1,0:T(8,128)(2,1)}) %all-gather.8.cloned.1.call-update) | async-done | bytes 2097168 | tf_op jit(solution)/shard_map/all_gather | solution.py:20
  89.7 7.7 %convert_reduce_fusion.5 = (f32[128]{0:T(128)S(1)}, bf16[128,512]{1,0:T(8,128)(2,1)}, f32[128,512]{1,0:T(8,128)}) fusion(f32[512,128,8]{0,1,2:T(8,128)S(1)} %get-tuple-element.18, f32[128]{0:T(128)S(1)} %psum.56, bf16[128,8192]{1,0:T(8,128)(2,1)} %all-gather.8.cloned.1.call-done, bf16[512,8192]{1,0:T(8,128)(2,1)} %param.6), kind=kOutput, calls=%fused_computation.69 | convolution fusion | flops 1074069376 | bytes 11142144 | tf_op jit(solution)/shard_map/dot_general | solution.py:22
  97.4 32.3 %psum.57 = f32[128]{0:T(128)S(1)} all-reduce(f32[128]{0:T(128)S(1)} %get-tuple-element.16), channel_id=1, replica_groups=mesh['groups'=2,'state'=16] {'state'}, use_global_device_ids=true, to_apply=%region_3.4 | all-reduce | flops 128 | bytes 1024 | tf_op jit(solution)/shard_map/psum | solution.py:21
  129.7 8.1 %all-gather.10.cloned.1.call-done = bf16[128,8192]{1,0:T(8,128)(2,1)} async-done(((bf16[128,512]{1,0:T(8,128)(2,1)}), bf16[128,8192]{1,0:T(8,128)(2,1)}) %all-gather.10.cloned.1.call-update) | async-done | bytes 2097168 | tf_op jit(solution)/shard_map/all_gather | solution.py:20
  137.8 7.7 %convert_reduce_fusion.4 = (f32[128]{0:T(128)S(1)}, bf16[128,512]{1,0:T(8,128)(2,1)}, f32[128,512]{1,0:T(8,128)}) fusion(f32[512,128,8]{0,1,2:T(8,128)S(1)} %get-tuple-element.18, f32[128]{0:T(128)S(1)} %psum.57, bf16[128,8192]{1,0:T(8,128)(2,1)} %all-gather.10.cloned.1.call-done, bf16[512,8192]{1,0:T(8,128)(2,1)} %param.6), kind=kOutput, calls=%fused_computation.68 | convolution fusion | flops 1074069376 | bytes 11142144 | tf_op jit(solution)/shard_map/dot_general | solution.py:22
  145.6 31.7 %psum.58 = f32[128]{0:T(128)S(1)} all-reduce(f32[128]{0:T(128)S(1)} %get-tuple-element.14), channel_id=1, replica_groups=mesh['groups'=2,'state'=16] {'state'}, use_global_device_ids=true, to_apply=%region_5.6 | all-reduce | flops 128 | bytes 1024 | tf_op jit(solution)/shard_map/psum | solution.py:21
  177.3 8.5 %all-gather.12.cloned.1.call-done = bf16[128,8192]{1,0:T(8,128)(2,1)} async-done(((bf16[128,512]{1,0:T(8,128)(2,1)}), bf16[128,8192]{1,0:T(8,128)(2,1)}) %all-gather.12.cloned.1.call-update) | async-done | bytes 2097168 | tf_op jit(solution)/shard_map/all_gather | solution.py:20
  185.9 7.7 %convert_reduce_fusion.3 = (f32[128]{0:T(128)S(1)}, bf16[128,512]{1,0:T(8,128)(2,1)}, f32[128,512]{1,0:T(8,128)}) fusion(f32[512,128,8]{0,1,2:T(8,128)S(1)} %get-tuple-element.18, f32[128]{0:T(128)S(1)} %psum.58, bf16[128,8192]{1,0:T(8,128)(2,1)} %all-gather.12.cloned.1.call-done, bf16[512,8192]{1,0:T(8,128)(2,1)} %param.6), kind=kOutput, calls=%fused_computation.67 | convolution fusion | flops 1074069376 | bytes 11142144 | tf_op jit(solution)/shard_map/dot_general | solution.py:22
  193.6 32.3 %psum.59 = f32[128]{0:T(128)S(1)} all-reduce(f32[128]{0:T(128)S(1)} %get-tuple-element.12), channel_id=1, replica_groups=mesh['groups'=2,'state'=16] {'state'}, use_global_device_ids=true, to_apply=%region_7.8 | all-reduce | flops 128 | bytes 1024 | tf_op jit(solution)/shard_map/psum | solution.py:21
  226.0 8.0 %all-gather.14.cloned.1.call-done = bf16[128,8192]{1,0:T(8,128)(2,1)} async-done(((bf16[128,512]{1,0:T(8,128)(2,1)}), bf16[128,8192]{1,0:T(8,128)(2,1)}) %all-gather.14.cloned.1.call-update) | async-done | bytes 2097168 | tf_op jit(solution)/shard_map/all_gather | solution.py:20
  233.9 7.7 %convert_reduce_fusion.2 = (f32[128]{0:T(128)S(1)}, bf16[128,512]{1,0:T(8,128)(2,1)}, f32[128,512]{1,0:T(8,128)}) fusion(f32[512,128,8]{0,1,2:T(8,128)S(1)} %get-tuple-element.18, f32[128]{0:T(128)S(1)} %psum.59, bf16[128,8192]{1,0:T(8,128)(2,1)} %all-gather.14.cloned.1.call-done, bf16[512,8192]{1,0:T(8,128)(2,1)} %param.6), kind=kOutput, calls=%fused_computation.66 | convolution fusion | flops 1074069376 | bytes 11142144 | tf_op jit(solution)/shard_map/dot_general | solution.py:22
  241.7 32.2 %psum.60 = f32[128]{0:T(128)S(1)} all-reduce(f32[128]{0:T(128)S(1)} %get-tuple-element.10), channel_id=1, replica_groups=mesh['groups'=2,'state'=16] {'state'}, use_global_device_ids=true, to_apply=%region_9.10 | all-reduce | flops 128 | bytes 1024 | tf_op jit(solution)/shard_map/psum | solution.py:21
  273.9 8.1 %all-gather.16.cloned.1.call-done = bf16[128,8192]{1,0:T(8,128)(2,1)} async-done(((bf16[128,512]{1,0:T(8,128)(2,1)}), bf16[128,8192]{1,0:T(8,128)(2,1)}) %all-gather.16.cloned.1.call-update) | async-done | bytes 2097168 | tf_op jit(solution)/shard_map/all_gather | solution.py:20
  282.0 7.7 %convert_reduce_fusion.1 = (f32[128]{0:T(128)S(1)}, bf16[128,512]{1,0:T(8,128)(2,1)}, f32[128,512]{1,0:T(8,128)}) fusion(f32[512,128,8]{0,1,2:T(8,128)S(1)} %get-tuple-element.18, f32[128]{0:T(128)S(1)} %psum.60, bf16[128,8192]{1,0:T(8,128)(2,1)} %all-gather.16.cloned.1.call-done, bf16[512,8192]{1,0:T(8,128)(2,1)} %param.6), kind=kOutput, calls=%fused_computation.65 | convolution fusion | flops 1074069376 | bytes 11142144 | tf_op jit(solution)/shard_map/dot_general | solution.py:22
  289.8 32.1 %psum.61 = f32[128]{0:T(128)S(1)} all-reduce(f32[128]{0:T(128)S(1)} %get-tuple-element.8), channel_id=1, replica_groups=mesh['groups'=2,'state'=16] {'state'}, use_global_device_ids=true, to_apply=%region_11.12 | all-reduce | flops 128 | bytes 1024 | tf_op jit(solution)/shard_map/psum | solution.py:21
  321.9 8.1 %all-gather.18.cloned.1.call-done = bf16[128,8192]{1,0:T(8,128)(2,1)} async-done(((bf16[128,512]{1,0:T(8,128)(2,1)}), bf16[128,8192]{1,0:T(8,128)(2,1)}) %all-gather.18.cloned.1.call-update) | async-done | bytes 2097168 | tf_op jit(solution)/shard_map/all_gather | solution.py:20
  330.0 7.6 %convert_reduce_fusion = (f32[128]{0:T(128)S(1)}, bf16[128,512]{1,0:T(8,128)(2,1)}, f32[128,512]{1,0:T(8,128)}) fusion(f32[512,128,8]{0,1,2:T(8,128)} %copy-done.8, f32[128]{0:T(128)S(1)} %psum.61, bf16[128,8192]{1,0:T(8,128)(2,1)} %all-gather.18.cloned.1.call-done, bf16[512,8192]{1,0:T(8,128)(2,1)} %param.6), kind=kOutput, calls=%fused_computation.64 | convolution fusion | flops 1074069376 | bytes 11142144 | tf_op jit(solution)/shard_map/dot_general | solution.py:22
  337.7 1.9 fusion.42
  339.7 32.0 %psum.62 = f32[128]{0:T(128)S(1)} all-reduce(f32[128]{0:T(128)S(1)} %get-tuple-element.6), channel_id=1, replica_groups=mesh['groups'=2,'state'=16] {'state'}, use_global_device_ids=true, to_apply=%region_13.14 | all-reduce | flops 128 | bytes 1024 | tf_op jit(solution)/shard_map/psum | solution.py:21
  371.7 6.4 %all-gather.20.cloned.1.call-done = bf16[128,8192]{1,0:T(8,128)(2,1)} async-done(((bf16[128,512]{1,0:T(8,128)(2,1)}), bf16[128,8192]{1,0:T(8,128)(2,1)}) %all-gather.20.cloned.1.call-update) | async-done | bytes 2097168 | tf_op jit(solution)/shard_map/all_gather | solution.py:20
  378.1 7.7 %constant_dynamic-update-slice_fusion.1 = (f32[128,7,512]{2,0,1:T(8,128)S(1)}, f32[128,8,512]{2,0,1:T(8,128)}) fusion(f32[128]{0:T(128)S(1)} %psum.62, bf16[128,8192]{1,0:T(8,128)(2,1)} %all-gather.20.cloned.1.call-done, bf16[512,8192]{1,0:T(8,128)(2,1)} %param.6), kind=kOutput, calls=%fused_computation.81 | convolution fusion | flops 1073807360 | bytes 11010560 | tf_op jit(solution)/shard_map/dot_general | solution.py:22
  385.9 0.7 bitcast_dynamic-update-slice_fusion.10
  386.6 0.7 bitcast_dynamic-update-slice_fusion.8
  389.6 0.7 bitcast_dynamic-update-slice_fusion
  390.4 1.2 fusion
  391.5 31.5 %psum.63 = f32[128,7]{0,1:T(8,128)S(1)} all-reduce(f32[128,7]{0,1:T(8,128)S(1)} %fusion), channel_id=1, replica_groups=mesh['groups'=2,'state'=16] {'state'}, use_global_device_ids=true, to_apply=%region_15.16 | all-reduce | flops 896 | bytes 7168 | tf_op jit(solution)/shard_map/psum | solution.py:38
  423.8 4.2 copy.26
  428.7 0.9 copy-done.6
  429.6 1.5 constant_dynamic-update-slice_fusion.8
  431.1 0.9 copy-done.5
  431.9 1.5 constant_dynamic-update-slice_fusion.7
  433.4 0.9 copy-done.4
  434.3 1.5 constant_dynamic-update-slice_fusion.6
  435.8 0.9 copy-done.3
  436.6 1.5 constant_dynamic-update-slice_fusion.5
  438.1 1.5 constant_dynamic-update-slice_fusion.4
  439.6 1.3 copy-done.1
  440.9 1.5 constant_dynamic-update-slice_fusion.3
  442.4 1.5 constant_dynamic-update-slice_fusion.2
  443.9 0.8 slice-done.1
  444.6 15.9 %multiply_multiply_fusion = f32[512,8192]{1,0:T(8,128)} fusion(bf16[512,8192]{1,0:T(8,128)(2,1)S(1)} %bitcast.172, bf16[896,512]{1,0:T(8,128)(2,1)S(1)} %fusion.34, bf16[896,8192]{1,0:T(8,128)(2,1)} %constant_dynamic-update-slice_fusion.2), kind=kOutput, calls=%fused_computation.1 | convolution fusion | flops 7528775680 | bytes 40763392 | tf_op jit(solution)/shard_map/dot_general | solution.py:46
  (65 shorter events, 5.6 us)
Async XLA Ops:
  7.2 82.5 %all-gather.8.cloned.1.call-start = ((), (), s32[]{:S(2)}) async-start(), calls=%async_computation | async-start | bytes 2228224 | tf_op jit(solution)/shard_map/all_gather | solution.py:20
  43.9 1.0 copy-start.9
  43.9 238.1 %copy-start.8 = (f32[512,128,8]{0,1,2:T(8,128)}, f32[512,128,8]{0,1,2:T(8,128)S(1)}, u32[]{:S(2)}) copy-start(f32[512,128,8]{0,1,2:T(8,128)S(1)} %get-tuple-element.18) | copy-start | bytes 6291460
  45.6 92.2 %all-gather.10.cloned.1.call-start = ((), (), s32[]{:S(2)}) async-start(), calls=%async_computation.1 | async-start | bytes 2228224 | tf_op jit(solution)/shard_map/all_gather | solution.py:20
  97.4 88.5 %all-gather.12.cloned.1.call-start = ((), (), s32[]{:S(2)}) async-start(), calls=%async_computation.2 | async-start | bytes 2228224 | tf_op jit(solution)/shard_map/all_gather | solution.py:20
  145.6 88.4 %all-gather.14.cloned.1.call-start = ((), (), s32[]{:S(2)}) async-start(), calls=%async_computation.3 | async-start | bytes 2228224 | tf_op jit(solution)/shard_map/all_gather | solution.py:20
  193.6 88.4 %all-gather.16.cloned.1.call-start = ((), (), s32[]{:S(2)}) async-start(), calls=%async_computation.4 | async-start | bytes 2228224 | tf_op jit(solution)/shard_map/all_gather | solution.py:20
  241.6 88.4 %all-gather.18.cloned.1.call-start = ((), (), s32[]{:S(2)}) async-start(), calls=%async_computation.5 | async-start | bytes 2228224 | tf_op jit(solution)/shard_map/all_gather | solution.py:20
  289.7 88.4 %all-gather.20.cloned.1.call-start = ((), (), s32[]{:S(2)}) async-start(), calls=%async_computation.6 | async-start | bytes 2228224 | tf_op jit(solution)/shard_map/all_gather | solution.py:20
  321.9 15.8 %copy-start.7 = (f32[128,8,512]{2,1,0:T(8,128)S(1)}, f32[128,8,512]{2,1,0:T(8,128)}, u32[]{:S(2)}) copy-start(f32[128,8,512]{2,1,0:T(8,128)} %param.4) | copy-start | bytes 6291460
  378.1 7.7 %copy-start.17 = (f32[128,512]{1,0:T(8,128)S(1)}, f32[128,512]{1,0:T(8,128)}, u32[]{:S(2)}) copy-start(f32[128,512]{1,0:T(8,128)} %get-tuple-element.53) | copy-start | bytes 786436
  378.1 8.5 %copy-start.16 = (f32[128,512]{1,0:T(8,128)S(1)}, f32[128,512]{1,0:T(8,128)}, u32[]{:S(2)}) copy-start(f32[128,512]{1,0:T(8,128)} %get-tuple-element.52) | copy-start | bytes 786436
  378.1 9.2 %copy-start.15 = (f32[128,512]{1,0:T(8,128)S(1)}, f32[128,512]{1,0:T(8,128)}, u32[]{:S(2)}) copy-start(f32[128,512]{1,0:T(8,128)} %get-tuple-element.51) | copy-start | bytes 786436
  385.9 2.3 copy-start.14
  385.9 3.0 copy-start.13
  385.9 3.7 copy-start.12
  423.8 4.2 copy-start.11
  423.8 4.3 copy-start.10
  428.0 1.6 copy-start.6
  429.6 2.3 copy-start.5
  431.9 2.3 copy-start.4
  434.3 2.3 copy-start.3
  434.3 3.8 copy-start.2
  436.6 7.3 %slice-start = ((s8[8388608]{0:T(1024)(128)(4,1)}), s8[4194304]{0:T(1024)(128)(4,1)S(1)}, s32[]{:S(2)}) async-start(s8[8388608]{0:T(1024)(128)(4,1)} %bitcast.171), calls=%async_computation.7 | async-start | bytes 8388608
  438.1 2.8 copy-start.1
  438.1 4.3 copy-start
  440.9 3.7 slice-start.1
Sparse Core Ops, SparseCore 0:
  45.7 43.8 all-gather.7
  97.5 40.2 all-gather.9
  145.7 40.1 all-gather.11
  193.7 40.1 all-gather.13
  241.8 40.1 all-gather.15
  289.8 40.1 all-gather.17
  337.8 40.2 all-gather.19
where the time goes:
time: 468 us; the launch traced here: 467 us
  blocking collectives  260 us (56%)
  matrix products  69.7 us (15%)
  local copies, waits for them, and re-layouts  64.2 us (14%)
  waiting for transfers between devices  55 us (12%)
  between operations  14.3 us (3%)
    psum x7, blocking collectives, on_device(): scale_sum = lax.psum(jnp.sum(weighted.astype(jnp.float32), axis=1), 'state')  228 us
    all_gather x7, waiting for transfers between devices, on_device(): whole = lax.all_gather(weighted, 'state', axis=1, tiled=True)  54.9 us
    dot_general x7, matrix products, on_device(): lax.dot_general(whole, transition, (((1,), (1,)), ((), ())), preferred_el...  53.8 us
    unnamed x54, local copies, waits for them, and re-layouts  46.6 us
    psum x1, blocking collectives, on_device(): norm_sums = lax.psum(partial_norms, 'state')  31.5 us
    dot_general x1, matrix products, on_device(): lax.dot_general(share_mat, vector_mat, (((0,), (0,)), ((), ())), preferre...  15.9 us
    gather x1, local copies, waits for them, and re-layouts, on_device(): jnp.take(emission, token_ids.reshape(-1), axis=1).astype(jnp.float32)  11.9 us
  transfers between devices with their start and end apart: 7, of which 7 were waited for; matrix products, arithmetic and copies ran while one was open for 1% of the time, Pallas kernels for 0%

commit v1 on v0

--- a/solution.py
+++ b/solution.py
@@ -2,6 +2,37 @@
 import jax.numpy as jnp
 from jax import lax
 from jax.sharding import PartitionSpec as P
+
+
+def build_the_points(xin, ndim_at):
+    xin = jnp.moveaxis(xin, 0, ndim_at)
+    x_new = xin.shape
+    t_next = xin.reshape(
+        *x_new[:ndim_at], x_new[ndim_at] * x_new[ndim_at + 1], *x_new[ndim_at + 2 :]
+    )
+    return t_next
+
+
+def draft_wall(inp, ax_name, axis_k):
+    width = lax.axis_size(ax_name)
+    trail = [(m, (m + 1) % width) for m in range(width)]
+    rows = [(s, tick) for tick, s in trail]
+    all_values, v_next = ([], [])
+    for j in [*range(width - 1)]:
+        if j % 2 == 0:
+            u_next = lax.ppermute(
+                all_values[-1] if all_values else inp, axis_name=ax_name, perm=trail
+            )
+            all_values.append(u_next)
+        else:
+            v_next.append(lax.ppermute(v_next[-1] if v_next else inp, ax_name, perm=rows))
+    taken_in = jnp.stack([*all_values[::-1], inp, *v_next])
+    odd = lax.axis_index(ax_name)
+    d_next = len(all_values)
+    extra = odd - d_next
+    taken_in = taken_in[(jnp.arange(width) - extra) % width]
+    side_arr = build_the_points(taken_in, axis_k)
+    return side_arr
 
 
 def on_device(forward_probs, token_ids, transition, emission):
@@ -17,7 +48,7 @@
     stored = []
     scales = []
     for t in range(step_count - 2, -1, -1):
-        whole = lax.all_gather(weighted, "state", axis=1, tiled=True)
+        whole = draft_wall(weighted, "state", 1)
         scale_sum = lax.psum(jnp.sum(weighted.astype(jnp.float32), axis=1), "state")
         product = lax.dot_general(
             whole, transition, (((1,), (1,)), ((), ())), preferred_element_type=jnp.float32

time: 468 us -> 933 us (1.99)
  starting transfers between devices: 0.29 us -> 188 us
  local copies, waits for them, and re-layouts: 64.2 us -> 213 us
  waiting for transfers between devices: 55 us -> 163 us
  matrix products: 69.7 us -> 82.6 us
  between operations: 14.3 us -> 1.7 us
  blocking collectives: 260 us -> 271 us
    ppermute x0 -> x105, starting transfers between devices: none -> 188 us  [the longest x49 184 us: draft_wall(): lax.ppermute(v_next[-1] if v_next else inp, ax_name, perm=rows)]
    ppermute x0 -> x105, waiting for transfers between devices: none -> 163 us  [the longest x56 162 us: draft_wall(): lax.ppermute(all_values[-1] if all_values else inp, axis_name=ax_name, pe...]
    unnamed x54 -> x229, local copies, waits for them, and re-layouts: 46.6 us -> 142 us
    all_gather x7 -> x0, waiting for transfers between devices: 54.9 us -> none  [on_device(): whole = lax.all_gather(weighted, 'state', axis=1, tiled=True)]
    transpose x0 -> x7, local copies, waits for them, and re-layouts: none -> 26.5 us  [build_the_points(): xin = jnp.moveaxis(xin, 0, ndim_at)]
    gather x0 -> x7, local copies, waits for them, and re-layouts: none -> 23.5 us  [draft_wall(): taken_in = taken_in[(jnp.arange(width) - extra) % width]]
    psum x7, blocking collectives: 228 us -> 241 us  [on_device(): scale_sum = lax.psum(jnp.sum(weighted.astype(jnp.float32), axis=1), 'state')]
    dot_general x1, matrix products: 15.9 us -> 27.7 us  [on_device(): lax.dot_general(share_mat, vector_mat, (((0,), (0,)), ((), ())), preferre...]
  transfers between devices with their start and end apart: 7 -> 105, of which waited for: 7 -> 49; matrix products, arithmetic and copies ran while one was open for 1% -> 10% of each run, Pallas kernels for 0% -> 0%
where the time goes in v1:
time: 933 us; the launch traced here: 924 us
  blocking collectives  271 us (29%)
  local copies, waits for them, and re-layouts  213 us (23%)
  starting transfers between devices  188 us (20%)
  waiting for transfers between devices  163 us (17%)
  matrix products  82.6 us (9%)
    psum x7, blocking collectives, on_device(): scale_sum = lax.psum(jnp.sum(weighted.astype(jnp.float32), axis=1), 'state')  241 us
    ppermute x49, starting transfers between devices, draft_wall(): lax.ppermute(v_next[-1] if v_next else inp, ax_name, perm=rows)  184 us
    ppermute x56, waiting for transfers between devices, draft_wall(): lax.ppermute(all_values[-1] if all_values else inp, axis_name=ax_name, pe...  162 us
    unnamed x229, local copies, waits for them, and re-layouts  142 us
    dot_general x7, matrix products, on_device(): lax.dot_general(whole, transition, (((1,), (1,)), ((), ())), preferred_el...  54.9 us
    psum x1, blocking collectives, on_device(): norm_sums = lax.psum(partial_norms, 'state')  30 us
    dot_general x1, matrix products, on_device(): lax.dot_general(share_mat, vector_mat, (((0,), (0,)), ((), ())), preferre...  27.7 us
    transpose x7, local copies, waits for them, and re-layouts, build_the_points(): xin = jnp.moveaxis(xin, 0, ndim_at)  26.5 us
  transfers between devices with their start and end apart: 105, of which 49 were waited for; matrix products, arithmetic and copies ran while one was open for 10% of the time, Pallas kernels for 0%

profile of v1, /device:TPU:0, one launch (start us, length us, event | category | flops | bytes accessed | tf_op | source)
XLA Modules:
  0.0 923.6 jit_solution(13781346332803504860)
XLA Ops:
  2.2 22.4 %copy.16 = bf16[512,16384]{0,1:T(8,128)(2,1)} copy(bf16[512,16384]{1,0:T(8,128)(2,1)} %param.7) | data formatting | bytes 33554432 | tf_op args[3]
  24.7 11.9 %gather_fusion = bf16[1024,512]{1,0:T(8,128)(2,1)S(1)} fusion(bf16[512,16384]{0,1:T(8,128)(2,1)} %copy.16, s32[1024]{0:T(1024)S(1)} %broadcast_clamp_fusion), kind=kCustom, calls=%fused_computation | custom fusion | bytes 2101248 | tf_op jit(solution)/shard_map/jit(_take)/gather | solution.py:43
  39.2 7.6 collective-permute-done
  46.8 4.4 collective-permute-start.8
  53.9 4.5 collective-permute-start.9
  82.9 4.5 collective-permute-start.13
  89.9 34.0 %psum.56 = f32[128]{0:T(128)S(1)} all-reduce(f32[128]{0:T(128)S(1)} %convert_reduce_fusion.6), channel_id=1, replica_groups=mesh['groups'=2,'state'=16] {'state'}, use_global_device_ids=true, to_apply=%region_1.2 | all-reduce | flops 128 | bytes 1024 | tf_op jit(solution)/shard_map/psum | solution.py:52
  135.9 7.0 convert_reduce_fusion.5
  143.4 6.6 collective-permute-done.15
  157.2 4.4 collective-permute-start.24
  164.4 4.4 collective-permute-start.25
  171.6 4.4 collective-permute-start.26
  178.8 4.4 collective-permute-start.27
  193.2 34.0 %psum.57 = f32[128]{0:T(128)S(1)} all-reduce(f32[128]{0:T(128)S(1)} %get-tuple-element.16), channel_id=1, replica_groups=mesh['groups'=2,'state'=16] {'state'}, use_global_device_ids=true, to_apply=%region_3.4 | all-reduce | flops 128 | bytes 1024 | tf_op jit(solution)/shard_map/psum | solution.py:52
  249.5 8.1 convert_reduce_fusion.4
  258.1 6.6 collective-permute-done.30
  271.9 4.4 collective-permute-start.39
  279.1 4.4 collective-permute-start.40
  286.3 4.4 collective-permute-start.41
  293.5 4.4 collective-permute-start.42
  307.9 34.1 %psum.58 = f32[128]{0:T(128)S(1)} all-reduce(f32[128]{0:T(128)} %get-tuple-element.14), channel_id=1, replica_groups=mesh['groups'=2,'state'=16] {'state'}, use_global_device_ids=true, to_apply=%region_5.6 | all-reduce | flops 128 | bytes 1024 | tf_op jit(solution)/shard_map/psum | solution.py:52
  363.9 8.1 convert_reduce_fusion.3
  372.5 6.6 collective-permute-done.45
  386.3 4.4 collective-permute-start.54
  393.5 4.4 collective-permute-start.55
  400.7 4.4 collective-permute-start.56
  407.9 4.4 collective-permute-start.57
  422.3 34.7 %psum.59 = f32[128]{0:T(128)} all-reduce(f32[128]{0:T(128)} %get-tuple-element.12), channel_id=1, replica_groups=mesh['groups'=2,'state'=16] {'state'}, use_global_device_ids=true, to_apply=%region_7.8 | all-reduce | flops 128 | bytes 1024 | tf_op jit(solution)/shard_map/psum | solution.py:52
  478.7 8.1 convert_reduce_fusion.2
  487.3 6.6 collective-permute-done.60
  501.1 4.4 collective-permute-start.69
  508.3 4.4 collective-permute-start.70
  522.9 4.4 collective-permute-start.72
  537.3 34.7 %psum.60 = f32[128]{0:T(128)} all-reduce(f32[128]{0:T(128)} %get-tuple-element.10), channel_id=1, replica_groups=mesh['groups'=2,'state'=16] {'state'}, use_global_device_ids=true, to_apply=%region_9.10 | all-reduce | flops 128 | bytes 1024 | tf_op jit(solution)/shard_map/psum | solution.py:52
  593.8 8.1 convert_reduce_fusion.1
  602.4 6.6 collective-permute-done.75
  616.2 4.4 collective-permute-start.84
  623.4 4.4 collective-permute-start.85
  630.6 4.4 collective-permute-start.86
  637.8 4.4 collective-permute-start.87
  652.2 34.7 %psum.61 = f32[128]{0:T(128)} all-reduce(f32[128]{0:T(128)} %get-tuple-element.8), channel_id=1, replica_groups=mesh['groups'=2,'state'=16] {'state'}, use_global_device_ids=true, to_apply=%region_11.12 | all-reduce | flops 128 | bytes 1024 | tf_op jit(solution)/shard_map/psum | solution.py:52
  708.7 8.3 convert_reduce_fusion
  717.5 6.6 collective-permute-done.90
  760.1 4.5 collective-permute-start.103
  769.3 34.5 %psum.62 = f32[128]{0:T(128)} all-reduce(f32[128]{0:T(128)} %get-tuple-element.6), channel_id=1, replica_groups=mesh['groups'=2,'state'=16] {'state'}, use_global_device_ids=true, to_apply=%region_13.14 | all-reduce | flops 128 | bytes 1024 | tf_op jit(solution)/shard_map/psum | solution.py:52
  834.6 7.1 constant_dynamic-update-slice_fusion.126
  847.5 30.0 %psum.63 = f32[128,7]{0,1:T(8,128)S(1)} all-reduce(f32[128,7]{0,1:T(8,128)S(1)} %fusion), channel_id=1, replica_groups=mesh['groups'=2,'state'=16] {'state'}, use_global_device_ids=true, to_apply=%region_15.16 | all-reduce | flops 896 | bytes 7168 | tf_op jit(solution)/shard_map/psum | solution.py:69
  895.7 27.7 %multiply_multiply_fusion = f32[512,8192]{1,0:T(8,128)} fusion(bf16[512,8192]{1,0:T(8,128)(2,1)} %param.6, bf16[896,512]{1,0:T(8,128)(2,1)S(1)} %constant_dynamic-update-slice_fusion.127, bf16[896,8192]{0,1:T(8,128)(2,1)} %constant_dynamic-update-slice_fusion.134), kind=kOutput, calls=%fused_computation.8 | convolution fusion | flops 7528775680 | bytes 40763392 | tf_op jit(solution)/shard_map/dot_general | solution.py:77
  (451 shorter events, 384.6 us)
Async XLA Ops:
  38.7 8.2 collective-permute-start
  53.9 7.2 collective-permute-start.2
  53.9 7.2 collective-permute-start.9
  75.5 7.3 collective-permute-start.12
  82.9 41.0 %collective-permute-start.13 = (bf16[128,512]{1,0:T(8,128)(2,1)S(1)}, bf16[128,512]{1,0:T(8,128)(2,1)}, u32[]{:S(2)}, u32[]{:S(2)}) collective-permute-start(bf16[128,512]{1,0:T(8,128)(2,1)S(1)} %collective-permute-done.12), channel_id=1, source_target_pairs={{1,0},{2,1},{3,2},{4,3},{5,4},{6,5},{7,6},{8,7},{9,8},{10,9},{11,1... | collective-permute-start | bytes 393224 | tf_op jit(solution)/shard_map/ppermute | solution.py:28
  89.9 34.2 %collective-permute-start.7 = (bf16[128,512]{1,0:T(8,128)(2,1)S(1)}, bf16[128,512]{1,0:T(8,128)(2,1)}, u32[]{:S(2)}, u32[]{:S(2)}) collective-permute-start(bf16[128,512]{1,0:T(8,128)(2,1)S(1)} %collective-permute-done.6), channel_id=1, source_target_pairs={{0,1},{1,2},{2,3},{3,4},{4,5},{5,6},{6,7},{7,8},{8,9},{9,10},{10,1... | collective-permute-start | bytes 393224 | tf_op jit(solution)/shard_map/ppermute | solution.py:23
  150.0 7.2 collective-permute-start.23
  157.2 7.2 collective-permute-start.17
  157.2 7.2 collective-permute-start.24
  178.8 7.2 collective-permute-start.27
  186.0 7.2 collective-permute-start.21
  186.6 40.6 %collective-permute-start.28 = (bf16[128,512]{1,0:T(8,128)(2,1)S(1)}, bf16[128,512]{1,0:T(8,128)(2,1)}, u32[]{:S(2)}, u32[]{:S(2)}) collective-permute-start(bf16[128,512]{1,0:T(8,128)(2,1)S(1)} %collective-permute-done.27), channel_id=1, source_target_pairs={{1,0},{2,1},{3,2},{4,3},{5,4},{6,5},{7,6},{8,7},{9,8},{10,9},{11,1... | collective-permute-start | bytes 393224 | tf_op jit(solution)/shard_map/ppermute | solution.py:28
  193.2 34.5 %collective-permute-start.22 = (bf16[128,512]{1,0:T(8,128)(2,1)}, bf16[128,512]{1,0:T(8,128)(2,1)}, u32[]{:S(2)}, u32[]{:S(2)}) collective-permute-start(bf16[128,512]{1,0:T(8,128)(2,1)} %collective-permute-done.21), channel_id=1, source_target_pairs={{0,1},{1,2},{2,3},{3,4},{4,5},{5,6},{6,7},{7,8},{8,9},{9,10},{10,1... | collective-permute-start | bytes 393224 | tf_op jit(solution)/shard_map/ppermute | solution.py:23
  227.2 14.1 %collective-permute-start.29 = (bf16[128,512]{1,0:T(8,128)(2,1)}, bf16[128,512]{1,0:T(8,128)(2,1)S(1)}, u32[]{:S(2)}, u32[]{:S(2)}) collective-permute-start(bf16[128,512]{1,0:T(8,128)(2,1)} %collective-permute-done.28), channel_id=1, source_target_pairs={{1,0},{2,1},{3,2},{4,3},{5,4},{6,5},{7,6},{8,7},{9,8},{10,9},{11,1... | collective-permute-start | bytes 393224 | tf_op jit(solution)/shard_map/ppermute | solution.py:28
  264.7 7.2 collective-permute-start.38
  293.5 7.2 collective-permute-start.35
  293.5 7.2 collective-permute-start.42
  300.7 7.2 collective-permute-start.36
  301.3 40.7 %collective-permute-start.43 = (bf16[128,512]{1,0:T(8,128)(2,1)S(1)}, bf16[128,512]{1,0:T(8,128)(2,1)}, u32[]{:S(2)}, u32[]{:S(2)}) collective-permute-start(bf16[128,512]{1,0:T(8,128)(2,1)S(1)} %collective-permute-done.42), channel_id=1, source_target_pairs={{1,0},{2,1},{3,2},{4,3},{5,4},{6,5},{7,6},{8,7},{9,8},{10,9},{11,1... | collective-permute-start | bytes 393224 | tf_op jit(solution)/shard_map/ppermute | solution.py:28
  307.9 34.2 %collective-permute-start.37 = (bf16[128,512]{1,0:T(8,128)(2,1)}, bf16[128,512]{1,0:T(8,128)(2,1)}, u32[]{:S(2)}, u32[]{:S(2)}) collective-permute-start(bf16[128,512]{1,0:T(8,128)(2,1)} %collective-permute-done.36), channel_id=1, source_target_pairs={{0,1},{1,2},{2,3},{3,4},{4,5},{5,6},{6,7},{7,8},{8,9},{9,10},{10,1... | collective-permute-start | bytes 393224 | tf_op jit(solution)/shard_map/ppermute | solution.py:23
  342.1 13.6 %collective-permute-start.44 = (bf16[128,512]{1,0:T(8,128)(2,1)}, bf16[128,512]{1,0:T(8,128)(2,1)S(1)}, u32[]{:S(2)}, u32[]{:S(2)}) collective-permute-start(bf16[128,512]{1,0:T(8,128)(2,1)} %collective-permute-done.43), channel_id=1, source_target_pairs={{1,0},{2,1},{3,2},{4,3},{5,4},{6,5},{7,6},{8,7},{9,8},{10,9},{11,1... | collective-permute-start | bytes 393224 | tf_op jit(solution)/shard_map/ppermute | solution.py:28
  379.1 7.2 collective-permute-start.53
  386.3 7.2 collective-permute-start.54
  407.9 7.2 collective-permute-start.57
  415.1 7.2 collective-permute-start.51
  415.7 41.3 %collective-permute-start.58 = (bf16[128,512]{1,0:T(8,128)(2,1)S(1)}, bf16[128,512]{1,0:T(8,128)(2,1)}, u32[]{:S(2)}, u32[]{:S(2)}) collective-permute-start(bf16[128,512]{1,0:T(8,128)(2,1)S(1)} %collective-permute-done.57), channel_id=1, source_target_pairs={{1,0},{2,1},{3,2},{4,3},{5,4},{6,5},{7,6},{8,7},{9,8},{10,9},{11,1... | collective-permute-start | bytes 393224 | tf_op jit(solution)/shard_map/ppermute | solution.py:28
  422.3 34.7 %collective-permute-start.52 = (bf16[128,512]{1,0:T(8,128)(2,1)}, bf16[128,512]{1,0:T(8,128)(2,1)}, u32[]{:S(2)}, u32[]{:S(2)}) collective-permute-start(bf16[128,512]{1,0:T(8,128)(2,1)} %collective-permute-done.51), channel_id=1, source_target_pairs={{0,1},{1,2},{2,3},{3,4},{4,5},{5,6},{6,7},{7,8},{8,9},{9,10},{10,1... | collective-permute-start | bytes 393224 | tf_op jit(solution)/shard_map/ppermute | solution.py:23
  457.0 13.6 %collective-permute-start.59 = (bf16[128,512]{1,0:T(8,128)(2,1)}, bf16[128,512]{1,0:T(8,128)(2,1)S(1)}, u32[]{:S(2)}, u32[]{:S(2)}) collective-permute-start(bf16[128,512]{1,0:T(8,128)(2,1)} %collective-permute-done.58), channel_id=1, source_target_pairs={{1,0},{2,1},{3,2},{4,3},{5,4},{6,5},{7,6},{8,7},{9,8},{10,9},{11,1... | collective-permute-start | bytes 393224 | tf_op jit(solution)/shard_map/ppermute | solution.py:28
  493.9 7.2 collective-permute-start.68
  508.3 7.2 collective-permute-start.63
  508.3 7.4 collective-permute-start.70
  515.5 7.4 collective-permute-start.64
  522.9 7.2 collective-permute-start.65
  522.9 7.2 collective-permute-start.72
  530.1 7.2 collective-permute-start.66
  530.7 41.3 %collective-permute-start.73 = (bf16[128,512]{1,0:T(8,128)(2,1)S(1)}, bf16[128,512]{1,0:T(8,128)(2,1)}, u32[]{:S(2)}, u32[]{:S(2)}) collective-permute-start(bf16[128,512]{1,0:T(8,128)(2,1)S(1)} %collective-permute-done.72), channel_id=1, source_target_pairs={{1,0},{2,1},{3,2},{4,3},{5,4},{6,5},{7,6},{8,7},{9,8},{10,9},{11,1... | collective-permute-start | bytes 393224 | tf_op jit(solution)/shard_map/ppermute | solution.py:28
  537.3 34.7 %collective-permute-start.67 = (bf16[128,512]{1,0:T(8,128)(2,1)}, bf16[128,512]{1,0:T(8,128)(2,1)}, u32[]{:S(2)}, u32[]{:S(2)}) collective-permute-start(bf16[128,512]{1,0:T(8,128)(2,1)} %collective-permute-done.66), channel_id=1, source_target_pairs={{0,1},{1,2},{2,3},{3,4},{4,5},{5,6},{6,7},{7,8},{8,9},{9,10},{10,1... | collective-permute-start | bytes 393224 | tf_op jit(solution)/shard_map/ppermute | solution.py:23
  572.0 13.6 %collective-permute-start.74 = (bf16[128,512]{1,0:T(8,128)(2,1)}, bf16[128,512]{1,0:T(8,128)(2,1)S(1)}, u32[]{:S(2)}, u32[]{:S(2)}) collective-permute-start(bf16[128,512]{1,0:T(8,128)(2,1)} %collective-permute-done.73), channel_id=1, source_target_pairs={{1,0},{2,1},{3,2},{4,3},{5,4},{6,5},{7,6},{8,7},{9,8},{10,9},{11,1... | collective-permute-start | bytes 393224 | tf_op jit(solution)/shard_map/ppermute | solution.py:28
  609.0 7.2 collective-permute-start.83
  637.8 7.2 collective-permute-start.87
  645.0 7.2 collective-permute-start.81
  645.7 41.3 %collective-permute-start.88 = (bf16[128,512]{1,0:T(8,128)(2,1)S(1)}, bf16[128,512]{1,0:T(8,128)(2,1)}, u32[]{:S(2)}, u32[]{:S(2)}) collective-permute-start(bf16[128,512]{1,0:T(8,128)(2,1)S(1)} %collective-permute-done.87), channel_id=1, source_target_pairs={{1,0},{2,1},{3,2},{4,3},{5,4},{6,5},{7,6},{8,7},{9,8},{10,9},{11,1... | collective-permute-start | bytes 393224 | tf_op jit(solution)/shard_map/ppermute | solution.py:28
  652.2 34.7 %collective-permute-start.82 = (bf16[128,512]{1,0:T(8,128)(2,1)}, bf16[128,512]{1,0:T(8,128)(2,1)}, u32[]{:S(2)}, u32[]{:S(2)}) collective-permute-start(bf16[128,512]{1,0:T(8,128)(2,1)} %collective-permute-done.81), channel_id=1, source_target_pairs={{0,1},{1,2},{2,3},{3,4},{4,5},{5,6},{6,7},{7,8},{8,9},{9,10},{10,1... | collective-permute-start | bytes 393224 | tf_op jit(solution)/shard_map/ppermute | solution.py:23
  686.9 13.6 %collective-permute-start.89 = (bf16[128,512]{1,0:T(8,128)(2,1)}, bf16[128,512]{1,0:T(8,128)(2,1)S(1)}, u32[]{:S(2)}, u32[]{:S(2)}) collective-permute-start(bf16[128,512]{1,0:T(8,128)(2,1)} %collective-permute-done.88), channel_id=1, source_target_pairs={{1,0},{2,1},{3,2},{4,3},{5,4},{6,5},{7,6},{8,7},{9,8},{10,9},{11,1... | collective-permute-start | bytes 393224 | tf_op jit(solution)/shard_map/ppermute | solution.py:28
  724.1 7.2 collective-permute-start.98
  760.1 43.8 %collective-permute-start.103 = (bf16[128,512]{1,0:T(8,128)(2,1)}, bf16[128,512]{1,0:T(8,128)(2,1)}, u32[]{:S(2)}, u32[]{:S(2)}) collective-permute-start(bf16[128,512]{1,0:T(8,128)(2,1)} %collective-permute-done.102), channel_id=1, source_target_pairs={{1,0},{2,1},{3,2},{4,3},{5,4},{6,5},{7,6},{8,7},{9,8},{10,9},{11,1... | collective-permute-start | bytes 393224 | tf_op jit(solution)/shard_map/ppermute | solution.py:28
  767.3 36.8 %collective-permute-start.97 = (bf16[128,512]{1,0:T(8,128)(2,1)}, bf16[128,512]{1,0:T(8,128)(2,1)}, u32[]{:S(2)}, u32[]{:S(2)}) collective-permute-start(bf16[128,512]{1,0:T(8,128)(2,1)} %collective-permute-done.96), channel_id=1, source_target_pairs={{0,1},{1,2},{2,3},{3,4},{4,5},{5,6},{6,7},{7,8},{8,9},{9,10},{10,1... | collective-permute-start | bytes 393224 | tf_op jit(solution)/shard_map/ppermute | solution.py:23
  803.9 19.3 %collective-permute-start.104 = (bf16[128,512]{1,0:T(8,128)(2,1)}, bf16[128,512]{1,0:T(8,128)(2,1)S(1)}, u32[]{:S(2)}, u32[]{:S(2)}) collective-permute-start(bf16[128,512]{1,0:T(8,128)(2,1)} %collective-permute-done.103), channel_id=1, source_target_pairs={{1,0},{2,1},{3,2},{4,3},{5,4},{6,5},{7,6},{8,7},{9,8},{10,9},{11,1... | collective-permute-start | bytes 393224 | tf_op jit(solution)/shard_map/ppermute | solution.py:28
  (112 other events, 1439.5 us)
